TPU v7x, 512 devices: a whole 4x8x8 slice. The times are simulated.
512 devices in a mesh: req: 64 (over y, x, core), tp: 8 (over z).
Axes of the slice: x: 4, y: 8, z: 8, core: 2. Of those that a mesh axis runs over, the one named last changes fastest.
Arguments:
- hidden: bfloat16 [2048, 5, 2560], P('req', None, 'tp'), may hold values from -6 to 6
- norm_gain: bfloat16 [2560], replicated, may hold values from 0.099609375 to 1.8984375
- query_weight: bfloat16 [2560, 2560], P(None, 'tp'), may hold values from -0.125 to 0.125
- key_value_matrix: bfloat16 [2560, 8, 160], P(None, 'tp'), may hold values from -0.125 to 0.125
- output_weight: bfloat16 [2560, 2560], P('tp'), may hold values from -0.5 to 0.5
- key_value_cache: bfloat16 [2048, 64, 8, 160], P('req', None, 'tp'), as said below
- deal_order: int32 [2048], P('req'), may hold values from 0 to 2047, as said below
- cache_length: int32 [2048], P('req'), may hold values from 1 to 64, as said below
- accepted: int32 [2048], P('req'), may hold values from 1 to 5
Outputs:
- block_output: bfloat16 [2048, 5, 2560], P('req', None, 'tp')
- new_entries: bfloat16 [2048, 5, 8, 160], P('req', None, 'tp')
Inputs may be any that keep to these rules, and one draw needn't show every extreme that they name: deal_order is a permutation of the 2048 requests; slot i lies on index i // 32 of req, and request r arrives on index r // 32. Every index deals at most 1 of its requests to any one index, and exactly 1 to each of 32 indices. Cache entries of slot i at positions from cache_length[i] on are unused. `key_value_cache`: at positions below cache_length[i] the first 80 entries of each head are the keys, already rotated for their positions, and the last 80 the values.
All inputs are finite; a program needn't handle non-finite values.
Results may differ from a plain program's by a relative error of at most 0.0091.
Values may be sent and summed in bfloat16 or wider, within the bound.
No kernel may reach another device: no remote copies, remote signals or barrier semaphores. Data moves between devices by JAX's collectives and lax.ppermute only.
A program may use at most 128 MiB of HBM per device.

v0:
```python
import math
import jax
import jax.numpy as jnp
from jax import lax
from jax.sharding import PartitionSpec as P

HEAD_SIZE = 80
masked_score = -1e30


def rotate(values, positions):
    half_dim = HEAD_SIZE // 2
    frequency = 10000.0 ** (-2.0 * jnp.arange(half_dim, dtype=jnp.float32) / HEAD_SIZE)
    angles = positions.astype(jnp.float32)[..., None] * frequency
    cosine_part = jnp.cos(angles)
    sine_part = jnp.sin(angles)
    first_half = values[..., :half_dim]
    second_half = values[..., half_dim:]
    return jnp.concatenate(
        [
            first_half * cosine_part - second_half * sine_part,
            second_half * cosine_part + first_half * sine_part,
        ],
        axis=-1,
    )


def attend(query_rows, key_value_cache, fresh, cache_length):
    scale = 1.0 / math.sqrt(HEAD_SIZE)
    slot_count = query_rows.shape[0]
    verified = query_rows.shape[1]
    cache_keys = key_value_cache[..., :HEAD_SIZE]
    cache_values = key_value_cache[..., HEAD_SIZE:]
    fresh_keys = fresh[..., :HEAD_SIZE]
    fresh_values = fresh[..., HEAD_SIZE:]
    cache_scores = (
        jnp.einsum("rtghd,rcgd->rghtc", query_rows, cache_keys, preferred_element_type=jnp.float32)
        * scale
    )
    visible = jnp.arange(key_value_cache.shape[1], dtype=jnp.int32)[None, :] < cache_length[:, None]
    cache_scores = jnp.where(visible[:, None, None, None, :], cache_scores, masked_score)
    fresh_scores = (
        jnp.einsum("rtghd,rugd->rghtu", query_rows, fresh_keys, preferred_element_type=jnp.float32)
        * scale
    )
    causal = (
        jnp.arange(verified, dtype=jnp.int32)[:, None]
        >= jnp.arange(verified, dtype=jnp.int32)[None, :]
    )
    fresh_scores = jnp.where(causal[None, None, None, :, :], fresh_scores, masked_score)
    largest = jnp.maximum(jnp.max(cache_scores, axis=-1), jnp.max(fresh_scores, axis=-1))[..., None]
    cache_expos = jnp.exp(cache_scores - largest)
    fresh_expos = jnp.exp(fresh_scores - largest)
    totals = jnp.sum(cache_expos, axis=-1, keepdims=True) + jnp.sum(
        fresh_expos, axis=-1, keepdims=True
    )
    cache_weights = (cache_expos / totals).astype(jnp.bfloat16)
    fresh_weights = (fresh_expos / totals).astype(jnp.bfloat16)
    mixed = jnp.einsum(
        "rghtc,rcgd->rtghd", cache_weights, cache_values, preferred_element_type=jnp.float32
    )
    mixed = mixed + jnp.einsum(
        "rghtu,rugd->rtghd", fresh_weights, fresh_values, preferred_element_type=jnp.float32
    )
    return mixed.astype(jnp.bfloat16).reshape(slot_count, verified, -1)


def body(
    hidden,
    norm_gain,
    query_weight,
    key_value_matrix,
    output_weight,
    key_value_cache,
    deal_order,
    cache_length,
    accepted,
):
    slot_count = deal_order.shape[0]
    verified = hidden.shape[1]
    device_index = lax.axis_index("req")
    my_requests = device_index * slot_count + jnp.arange(slot_count, dtype=jnp.int32)
    piece = lax.all_gather(hidden, "req", axis=0, tiled=True)
    picker = (deal_order[:, None] == jnp.arange(piece.shape[0], dtype=jnp.int32)[None, :]).astype(
        jnp.bfloat16
    )
    dealt_rows = jnp.einsum(
        "in,ntf->itf", picker, piece, preferred_element_type=jnp.float32
    ).astype(jnp.bfloat16)
    features = lax.all_gather(dealt_rows, "tp", axis=2, tiled=True)
    widened = features.astype(jnp.float32)
    variance = jnp.mean(widened * widened, axis=-1, keepdims=True)
    normed = (widened * lax.rsqrt(variance + 1e-05) * norm_gain.astype(jnp.float32)).astype(
        jnp.bfloat16
    )
    heads_here = query_weight.shape[1] // HEAD_SIZE
    groups_here = key_value_matrix.shape[1]
    positions = cache_length[:, None] + jnp.arange(verified, dtype=jnp.int32)[None, :]
    query_rows = jnp.einsum("rtd,de->rte", normed, query_weight, preferred_element_type=jnp.float32)
    query_rows = query_rows.reshape(
        slot_count, verified, groups_here, heads_here // groups_here, HEAD_SIZE
    )
    query_rows = rotate(query_rows, positions[:, :, None, None]).astype(jnp.bfloat16)
    projected = jnp.einsum(
        "rtd,dge->rtge", normed, key_value_matrix, preferred_element_type=jnp.float32
    )
    fresh = jnp.concatenate(
        [rotate(projected[..., :HEAD_SIZE], positions[:, :, None]), projected[..., HEAD_SIZE:]],
        axis=-1,
    ).astype(jnp.bfloat16)
    keep = (jnp.arange(verified, dtype=jnp.int32)[None, :] < accepted[:, None])[:, :, None, None]
    new_entries = jnp.where(keep, fresh, jnp.zeros_like(fresh))
    mixed = attend(query_rows, key_value_cache, fresh, cache_length)
    partial_sum = jnp.einsum(
        "rte,ed->rtd", mixed, output_weight, preferred_element_type=jnp.float32
    )
    out_dealt = lax.psum_scatter(partial_sum, "tp", scatter_dimension=2, tiled=True).astype(
        jnp.bfloat16
    )
    piece_rows = lax.all_gather(out_dealt, "req", axis=0, tiled=True)
    piece_owners = lax.all_gather(deal_order, "req", axis=0, tiled=True)
    picker = (my_requests[:, None] == piece_owners[None, :]).astype(jnp.bfloat16)
    block_output = jnp.einsum(
        "jn,ntf->jtf", picker, piece_rows, preferred_element_type=jnp.float32
    ).astype(jnp.bfloat16)
    return (block_output, new_entries)


def solution(mesh):
    placed = (
        P("req", None, "tp"),
        P(),
        P(None, "tp"),
        P(None, "tp", None),
        P("tp", None),
        P("req", None, "tp", None),
        P("req"),
        P("req"),
        P("req"),
    )
    return jax.shard_map(
        body,
        mesh=mesh,
        in_specs=placed,
        out_specs=(P("req", None, "tp"), P("req", None, "tp", None)),
        check_vma=False,
    )
```

profile of v0, /device:TPU:1, one launch (start us, length us, event | category | flops | bytes accessed | tf_op | source)
XLA Modules:
  0.0 338.5 jit_solution(15841835390689357700)
XLA Ops:
  7.2 0.0 copy-start
  7.2 0.0 all-gather.3.cloned.1.call-start
  7.2 0.7 all-gather.3.cloned.1.call-update
  7.9 0.0 reduce-scatter.4.cloned.1.call-start
  8.0 0.7 convert_element_type.71
  8.7 0.7 add_convert_fusion
  9.3 0.1 copy.46
  9.4 0.7 iota_compare_fusion.1
  10.2 0.5 multiply_cosine_fusion
  10.7 93.9 %all-gather.3.cloned.1.call-done = bf16[2048,5,320]{2,0,1:T(8,128)(2,1)} async-done(((bf16[32,5,320]{2,0,1:T(8,128)(2,1)}), bf16[2048,5,320]{2,0,1:T(8,128)(2,1)}) %all-gather.3.cloned.1.call-update) | async-done | bytes 6553616 | tf_op jit(solution)/shard_map/all_gather | solution.py:83
  104.6 4.7 %convolution_convert_fusion.1 = bf16[32,5,320]{2,0,1:T(8,128)(2,1)S(1)} fusion(bf16[2048,5,320]{2,0,1:T(8,128)(2,1)} %all-gather.3.cloned.1.call-done, s32[32]{0:T(128)} %param.15), kind=kOutput, calls=%fused_computation.21 | convolution fusion | flops 209831936 | bytes 6656128 | tf_op jit(solution)/shard_map/in,ntf->itf/dot_general | solution.py:87
  109.3 0.4 copy.43
  109.7 55.1 %all_gather.14 = bf16[32,5,2560]{0,1,2:T(8,128)(2,1)} all-gather(bf16[32,5,320]{0,1,2:T(8,128)(2,1)S(1)} %copy.43), channel_id=1, replica_groups=mesh['req'=64,'tp'=8] {'tp'}, dimensions={2}, use_global_device_ids=true | all-gather | bytes 921600 | tf_op jit(solution)/shard_map/all_gather | solution.py:90
  164.9 4.4 %copy.44 = bf16[32,5,2560]{2,0,1:T(8,128)(2,1)S(1)} copy(bf16[32,5,2560]{0,1,2:T(8,128)(2,1)} %all_gather.14) | data formatting | bytes 1638400 | tf_op jit(solution)/shard_map/all_gather | solution.py:90
  169.2 0.0 copy-start.4
  169.3 0.2 fusion
  169.5 1.7 convolution_bitcast_fusion.1
  171.2 0.0 copy-start.1
  171.2 0.1 slice_bitcast_fusion.4
  171.3 0.6 copy-done.1
  171.9 0.4 fusion.41
  172.3 0.0 copy-done.4
  172.3 0.8 fusion.5
  173.1 0.2 reshape.324
  173.3 0.2 fusion.49
  173.5 0.0 copy-start.2
  173.5 0.1 maximum_bitcast_fusion
  173.6 0.5 fusion.24
  174.1 1.4 fusion.51
  175.5 0.0 copy-done.2
  175.5 0.6 fusion.50
  176.1 0.3 fusion.22
  176.3 0.4 fusion.21
  176.8 0.8 convolution_bitcast_fusion
  177.6 0.4 fusion.13
  178.0 0.1 copy.53
  178.1 0.1 reshape.332
  178.2 0.0 copy-done
  178.2 0.6 fusion.3
  178.8 5.5 %copy.64 = f32[32,5,2560]{0,1,2:T(8,128)} copy(f32[32,5,2560]{2,0,1:T(8,128)S(1)} %fusion.3) | data formatting | bytes 3276800
  184.3 8.0 %reshape.347 = f32[2560,160]{1,0:T(8,128)} reshape(f32[2560,5,32]{2,1,0:T(8,128)} %bitcast.87) | data formatting | bytes 3276800
  192.4 0.0 copy-start.3
  192.4 0.0 copy-start.5
  192.4 0.0 reduce-scatter.4.cloned.1.call-update
  192.4 0.0 all-gather.5.cloned.1.call-start
  192.4 39.6 %reduce-scatter.4.cloned.1.call-done = f32[320,160]{1,0:T(8,128)} async-done(((f32[2560,160]{1,0:T(8,128)}), f32[320,160]{1,0:T(8,128)}) %reduce-scatter.4.cloned.1.call-update) | async-done | bytes 204816
  232.1 1.2 reshape.348
  233.3 1.0 copy.65
  234.3 0.0 all-gather.5.cloned.1.call-update
  234.3 1.3 dynamic-slice
  236.3 0.0 copy-done.3
  236.3 0.3 dynamic-update-slice
  236.5 21.3 %all-reduce = s32[2048]{0:T(1024)S(1)} all-reduce(s32[2048]{0:T(1024)S(1)} %dynamic-update-slice), channel_id=1, replica_groups=mesh['req'=64,'tp'=8] {'req'}, use_global_device_ids=true, to_apply=%add | all-reduce | flops 2048 | bytes 16384
  257.9 0.0 copy-done.5
  257.9 1.0 slice.51
  258.9 0.8 fusion.44
  259.7 67.0 %all-gather.5.cloned.1.call-done = bf16[2048,5,320]{2,0,1:T(8,128)(2,1)} async-done(((bf16[32,5,320]{2,0,1:T(8,128)(2,1)}), bf16[2048,5,320]{2,0,1:T(8,128)(2,1)}) %all-gather.5.cloned.1.call-update) | async-done | bytes 6553616 | tf_op jit(solution)/shard_map/all_gather | solution.py:120
  326.7 5.3 %convolution_convert_fusion = bf16[32,5,320]{2,0,1:T(8,128)(2,1)} fusion(bf16[2048,5,320]{2,0,1:T(8,128)(2,1)} %all-gather.5.cloned.1.call-done, s32[2048]{0:T(1024)S(1)} %all-reduce, s32[32]{0:T(128)S(1)} %iota_add_fusion), kind=kOutput, calls=%fused_computation.20 | convolution fusion | flops 209831936 | bytes 6664320 | tf_op jit(solution)/shard_map/jn,ntf->jtf/dot_general | solution.py:123
  (8 shorter events, 0.1 us)
Async XLA Ops:
  7.2 171.1 %copy-start = (bf16[320,2560]{1,0:T(8,128)(2,1)S(1)}, bf16[320,2560]{1,0:T(8,128)(2,1)}, u32[]{:S(2)}) copy-start(bf16[320,2560]{1,0:T(8,128)(2,1)} %param.13) | copy-start | bytes 4915204
  7.2 97.5 %all-gather.3.cloned.1.call-start = ((), (), s32[]{:S(2)}) async-start(), calls=%async_computation.1 | async-start | bytes 7987200 | tf_op jit(solution)/shard_map/all_gather | solution.py:83
  7.9 224.2 %reduce-scatter.4.cloned.1.call-start = ((), (), s32[]{:S(2)}) async-start(), calls=%async_computation.3 | async-start | bytes 2949120
  169.2 3.0 copy-start.4
  171.2 0.7 copy-start.1
  173.5 1.9 copy-start.2
  192.4 43.9 %copy-start.3 = (s32[32]{0:T(128)S(1)}, s32[32]{0:T(128)}, u32[]{:S(2)}) copy-start(s32[32]{0:T(128)} %param.15) | copy-start | bytes 388
  192.4 65.5 %copy-start.5 = (s32[32]{0:T(128)S(1)}, s32[32]{0:T(128)}, u32[]{:S(2)}) copy-start(s32[32]{0:T(128)} %param.17) | copy-start | bytes 388
  192.4 134.3 %all-gather.5.cloned.1.call-start = ((), (), s32[]{:S(2)}) async-start(), calls=%async_computation.2 | async-start | bytes 7987200 | tf_op jit(solution)/shard_map/all_gather | solution.py:120
Sparse Core Ops, SparseCore 0:
  11.3 93.2 all-gather.2
  192.5 39.5 reduce-scatter.3
  235.9 90.6 all-gather.4
where the time goes:
time: 339 us; the launch traced here: 338 us
  waiting for transfers between devices  201 us (59%)
  blocking collectives  76.4 us (23%)
  local copies, waits for them, and re-layouts  24.5 us (7%)
  matrix products  16.2 us (5%)
  between operations  14.6 us (4%)
  other arithmetic  5.35 us (2%)
    all_gather x1, waiting for transfers between devices, body(): piece = lax.all_gather(hidden, 'req', axis=0, tiled=True)  93.9 us
    all_gather x1, waiting for transfers between devices, body(): piece_rows = lax.all_gather(out_dealt, 'req', axis=0, tiled=True)  67 us
    all_gather x1, blocking collectives, body(): features = lax.all_gather(dealt_rows, 'tp', axis=2, tiled=True)  55.1 us
    unnamed x4, waiting for transfers between devices  40.3 us
    unnamed x1, blocking collectives  21.3 us
    unnamed x19, local copies, waits for them, and re-layouts  17.9 us
  transfers between devices with their start and end apart: 3, of which 3 were waited for; matrix products, arithmetic and copies ran while one was open for 2% of the time, Pallas kernels for 0%

commit v1 on v0

--- a/solution.py
+++ b/solution.py
@@ -117,7 +117,8 @@
     out_dealt = lax.psum_scatter(partial_sum, "tp", scatter_dimension=2, tiled=True).astype(
         jnp.bfloat16
     )
-    piece_rows = lax.all_gather(out_dealt, "req", axis=0, tiled=True)
+    copies = jnp.concatenate([out_dealt] * lax.axis_size("req"), axis=0)
+    piece_rows = lax.all_to_all(copies, "req", 0, 0, tiled=True)
     piece_owners = lax.all_gather(deal_order, "req", axis=0, tiled=True)
     picker = (my_requests[:, None] == piece_owners[None, :]).astype(jnp.bfloat16)
     block_output = jnp.einsum(

time: 339 us -> 594 us (1.75)
  blocking collectives: 76.4 us -> 333 us
  waiting for transfers between devices: 201 us -> 135 us
  local copies, waits for them, and re-layouts: 24.5 us -> 65.9 us
  starting transfers between devices: 0.12 us -> 14.6 us
    unnamed x1, blocking collectives: 21.3 us -> 278 us
    all_gather x1 -> x0, waiting for transfers between devices: 67 us -> none  [body(): piece_rows = lax.all_gather(out_dealt, 'req', axis=0, tiled=True)]
    concatenate x0 -> x2, local copies, waits for them, and re-layouts: none -> 40.6 us  [body(): copies = jnp.concatenate([out_dealt] * lax.axis_size('req'), axis=0)]
    all_to_all x0 -> x1, starting transfers between devices: none -> 14.5 us  [body(): piece_rows = lax.all_to_all(copies, 'req', 0, 0, tiled=True)]
    unnamed x19 -> x80, local copies, waits for them, and re-layouts: 17.9 us -> 18.7 us
    unnamed x4 -> x3, waiting for transfers between devices: 40.3 us -> 40.7 us
  transfers between devices with their start and end apart: 3 -> 3, of which waited for: 3 -> 2; matrix products, arithmetic and copies ran while one was open for 2% -> 1% of each run, Pallas kernels for 0% -> 0%
where the time goes in v1:
time: 594 us; the launch traced here: 591 us
  blocking collectives  333 us (56%)
  waiting for transfers between devices  135 us (23%)
  local copies, waits for them, and re-layouts  65.9 us (11%)
  matrix products  21.5 us (4%)
  between operations  15.4 us (3%)
  starting transfers between devices  14.6 us (2%)
    unnamed x1, blocking collectives  278 us
    all_gather x1, waiting for transfers between devices, body(): piece = lax.all_gather(hidden, 'req', axis=0, tiled=True)  93.9 us
    all_gather x1, blocking collectives, body(): features = lax.all_gather(dealt_rows, 'tp', axis=2, tiled=True)  55.1 us
    unnamed x3, waiting for transfers between devices  40.7 us
    concatenate x2, local copies, waits for them, and re-layouts, body(): copies = jnp.concatenate([out_dealt] * lax.axis_size('req'), axis=0)  40.6 us
    unnamed x80, local copies, waits for them, and re-layouts  18.7 us
    all_to_all x1, starting transfers between devices, body(): piece_rows = lax.all_to_all(copies, 'req', 0, 0, tiled=True)  14.5 us
  transfers between devices with their start and end apart: 3, of which 2 were waited for; matrix products, arithmetic and copies ran while one was open for 1% of the time, Pallas kernels for 0%

profile of v1, /device:TPU:1, one launch (start us, length us, event | category | flops | bytes accessed | tf_op | source)
XLA Modules:
  0.0 590.8 jit_solution(13840675870241050126)
XLA Ops:
  7.2 0.0 copy-start
  7.2 0.0 all-gather.2.cloned.1.call-start
  7.2 0.7 all-gather.2.cloned.1.call-update
  7.9 0.0 reduce-scatter.4.cloned.1.call-start
  8.0 0.7 convert_element_type.71
  8.7 0.7 add_convert_fusion
  9.3 0.1 copy.63
  9.4 0.7 iota_compare_fusion.1
  10.2 0.5 multiply_cosine_fusion
  10.7 93.9 %all-gather.2.cloned.1.call-done = bf16[2048,5,320]{2,0,1:T(8,128)(2,1)} async-done(((bf16[32,5,320]{2,0,1:T(8,128)(2,1)}), bf16[2048,5,320]{2,0,1:T(8,128)(2,1)}) %all-gather.2.cloned.1.call-update) | async-done | bytes 6553616 | tf_op jit(solution)/shard_map/all_gather | solution.py:83
  104.6 4.7 convolution_convert_fusion
  109.3 0.4 copy.60
  109.7 55.1 %all_gather.11 = bf16[32,5,2560]{0,1,2:T(8,128)(2,1)} all-gather(bf16[32,5,320]{0,1,2:T(8,128)(2,1)S(1)} %copy.60), channel_id=1, replica_groups=mesh['req'=64,'tp'=8] {'tp'}, dimensions={2}, use_global_device_ids=true | all-gather | bytes 921600 | tf_op jit(solution)/shard_map/all_gather | solution.py:90
  164.9 4.4 copy.61
  169.2 0.2 fusion.2
  169.5 1.6 convolution_bitcast_fusion.1
  171.1 0.0 copy-start.2
  171.1 0.1 slice_bitcast_fusion.4
  171.2 0.6 copy-done.2
  171.7 0.4 fusion.46
  172.1 2.2 fusion.7
  174.3 0.2 reshape.324
  174.6 0.2 fusion.54
  174.8 0.1 maximum_bitcast_fusion
  174.9 0.5 fusion.29
  175.4 1.4 fusion.56
  176.7 1.6 fusion.55
  178.4 0.3 fusion.27
  178.6 0.4 fusion.26
  179.1 1.8 convolution_bitcast_fusion
  180.9 0.4 fusion.15
  181.3 0.1 copy.70
  181.4 0.1 reshape.332
  181.5 0.0 copy-done
  181.5 0.6 fusion.5
  182.1 5.5 copy.83
  187.6 8.0 %reshape.347 = f32[2560,160]{1,0:T(8,128)} reshape(f32[2560,5,32]{2,1,0:T(8,128)} %bitcast.86) | data formatting | bytes 3276800
  195.6 0.0 reduce-scatter.4.cloned.1.call-update
  195.7 40.0 %reduce-scatter.4.cloned.1.call-done = f32[320,160]{1,0:T(8,128)} async-done(((f32[2560,160]{1,0:T(8,128)}), f32[320,160]{1,0:T(8,128)}) %reduce-scatter.4.cloned.1.call-update) | async-done | bytes 204816
  235.7 1.2 reshape.348
  236.9 0.3 copy.84
  239.1 40.5 %copy.71 = bf16[2048,5,320]{2,1,0:T(8,128)(2,1)} copy(bf16[2048,5,320]{2,0,1:T(8,128)(2,1)S(1)} %constant_dynamic-update-slice_fusion) | data formatting | bytes 13107200 | tf_op jit(solution)/shard_map/concatenate | solution.py:120
  279.7 0.0 copy-start.3
  279.7 0.0 copy-start.4
  279.7 14.5 %all-to-all-start = ((bf16[2048,5,320]{2,1,0:T(8,128)(2,1)}), bf16[2048,5,320]{2,1,0:T(8,128)(2,1)}, u32[]{:S(2)}, u32[]{:S(2)}) async-start(bf16[2048,5,320]{2,1,0:T(8,128)(2,1)} %copy.71), calls=%async_computation | async-start | bytes 25165824 | tf_op jit(solution)/shard_map/all_to_all | solution.py:121
  294.2 0.0 copy-start.1
  294.2 1.4 dynamic-slice
  296.3 0.0 copy-done.3
  296.3 0.3 dynamic-update-slice
  296.6 278.3 %all-reduce = s32[2048]{0:T(1024)S(1)} all-reduce(s32[2048]{0:T(1024)S(1)} %dynamic-update-slice), channel_id=1, replica_groups=mesh['req'=64,'tp'=8] {'req'}, use_global_device_ids=true, to_apply=%add | all-reduce | flops 2048 | bytes 16384
  574.9 0.0 copy-done.4
  574.9 1.0 slice.51
  575.9 0.8 fusion.49
  576.7 0.0 all-to-all-done
  576.7 7.3 %fusion.16 = bf16[32,5,320]{2,0,1:T(8,128)(2,1)} fusion(bf16[2048,5,320]{2,1,0:T(8,128)(2,1)} %all-to-all-done, s32[2048]{0:T(1024)S(1)} %all-reduce, s32[32]{0:T(128)S(1)} %iota_add_fusion), kind=kOutput, calls=%fused_computation.22 | convolution fusion | flops 209831936 | bytes 6664320 | tf_op jit(solution)/shard_map/jn,ntf->jtf/dot_general | solution.py:124
  584.0 0.0 copy-done.1
  (72 shorter events, 1.5 us)
Async XLA Ops:
  7.2 174.4 %copy-start = (bf16[320,2560]{1,0:T(8,128)(2,1)S(1)}, bf16[320,2560]{1,0:T(8,128)(2,1)}, u32[]{:S(2)}) copy-start(bf16[320,2560]{1,0:T(8,128)(2,1)} %param.13) | copy-start | bytes 4915204
  7.2 97.5 %all-gather.2.cloned.1.call-start = ((), (), s32[]{:S(2)}) async-start(), calls=%async_computation.2 | async-start | bytes 7987200 | tf_op jit(solution)/shard_map/all_gather | solution.py:83
  7.9 227.7 %reduce-scatter.4.cloned.1.call-start = ((), (), s32[]{:S(2)}) async-start(), calls=%async_computation.3 | async-start | bytes 2949120
  171.1 0.7 copy-start.2
  279.7 16.6 %copy-start.3 = (s32[32]{0:T(128)S(1)}, s32[32]{0:T(128)}, u32[]{:S(2)}) copy-start(s32[32]{0:T(128)} %param.15) | copy-start | bytes 388
  279.7 295.2 %copy-start.4 = (s32[32]{0:T(128)S(1)}, s32[32]{0:T(128)}, u32[]{:S(2)}) copy-start(s32[32]{0:T(128)} %param.17) | copy-start | bytes 388
  279.7 297.0 %all-to-all-start = ((bf16[2048,5,320]{2,1,0:T(8,128)(2,1)}), bf16[2048,5,320]{2,1,0:T(8,128)(2,1)}, u32[]{:S(2)}, u32[]{:S(2)}) async-start(bf16[2048,5,320]{2,1,0:T(8,128)(2,1)} %copy.71), calls=%async_computation | async-start | bytes 25165824 | tf_op jit(solution)/shard_map/all_to_all | solution.py:121
  294.2 289.7 %copy-start.1 = (bf16[320,2560]{1,0:T(8,128)(2,1)S(1)}, bf16[320,2560]{1,0:T(8,128)(2,1)}, u32[]{:S(2)}) copy-start(bf16[320,2560]{1,0:T(8,128)(2,1)} %param.13) | copy-start | bytes 4915204
Sparse Core Ops, SparseCore 0:
  11.3 93.2 all-gather.1
  195.8 39.8 reduce-scatter.3
